TPU v7x, 128 devices: a whole 4x4x4 slice. The times are simulated.
128 devices in a mesh: space: 32 (over x, z, core), feat: 4 (over y).
Axes of the slice: x: 4, y: 4, z: 4, core: 2. Of those that a mesh axis runs over, the one named last changes fastest.
Arguments:
- inputs: bfloat16 [2, 96, 180, 1024], P(None, 'space', None, 'feat'), may hold values from -15 to 15
- cotangent: bfloat16 [2, 96, 180, 1024], P(None, 'space', None, 'feat'), may hold values from -6 to 6
- spec_w1: float32 [2, 8, 128, 128], P(None, 'feat'), may hold values from -0.375 to 0.375
- spec_b1: float32 [2, 1024], P(None, 'feat'), may hold values from -0.3 to 0.3
- spec_w2: float32 [2, 8, 128, 128], P(None, 'feat'), may hold values from -0.375 to 0.375
- spec_b2: float32 [2, 1024], P(None, 'feat'), may hold values from -0.3 to 0.3
- up_weight: bfloat16 [1024, 4096], P(None, 'feat'), may hold values from -0.1875 to 0.1875
- down_weight: bfloat16 [4096, 1024], P('feat'), may hold values from -0.09375 to 0.09375
Outputs:
- output: bfloat16 [2, 96, 180, 1024], P(None, 'space', None, 'feat')
- grad_input: bfloat16 [2, 96, 180, 1024], P(None, 'space', None, 'feat')
All inputs are finite; a program needn't handle non-finite values.
Results may differ from a plain program's by a relative error of at most 0.0102.
Values may be sent and summed in bfloat16 or wider, within the bound.
No kernel may reach another device: no remote copies, remote signals or barrier semaphores. Data moves between devices by JAX's collectives and lax.ppermute only.
A program may use at most 128 MiB of HBM per device.

v0:
```python
import math
import jax
import jax.numpy as jnp
from jax import lax
from jax.sharding import PartitionSpec as P

EPSILON = 1e-05
SHRINK_LEVEL = 0.1
HIGHEST = lax.Precision.HIGHEST


def longitude_tables(width_lon):
    mode_count = width_lon // 2 + 1
    cell_index = jnp.arange(width_lon, dtype=jnp.int32)[:, None]
    wave_number = jnp.arange(mode_count, dtype=jnp.int32)[None, :]
    phase_angle = (
        2.0 * math.pi / width_lon * (cell_index * wave_number % width_lon).astype(jnp.float32)
    )
    scaling = 1.0 / math.sqrt(width_lon)
    cos_fwd = jnp.cos(phase_angle) * scaling
    sin_fwd = -jnp.sin(phase_angle) * scaling
    doubled = jnp.where((wave_number == 0) | (wave_number * 2 == width_lon), 1.0, 2.0).astype(
        jnp.float32
    )
    return (cos_fwd, sin_fwd, cos_fwd * doubled, sin_fwd * doubled)


def padded_tables(width_lon, multiple):
    tables = longitude_tables(width_lon)
    modes = tables[0].shape[1]
    extra = -modes % multiple
    return tuple((jnp.pad(table, ((0, 0), (0, extra))) for table in tables))


def lat_apply(table, field):
    return jnp.einsum("gh,bhkc->bgkc", table, field, precision=HIGHEST)


def complex_latitude(table_cos, table_sin, real_part, imag_part, inverse):
    if inverse:
        return (
            lat_apply(table_cos, real_part) + lat_apply(table_sin, imag_part),
            lat_apply(table_cos, imag_part) - lat_apply(table_sin, real_part),
        )
    return (
        lat_apply(table_cos, real_part) - lat_apply(table_sin, imag_part),
        lat_apply(table_cos, imag_part) + lat_apply(table_sin, real_part),
    )


def lon_forward(field, table):
    return jnp.einsum("brwc,wk->brkc", field, table, precision=HIGHEST)


def lon_back(spec, table):
    return jnp.einsum("brkc,wk->brwc", spec, table, precision=HIGHEST)


def to_blocks(field, block_size):
    return field.reshape(field.shape[:-1] + (field.shape[-1] // block_size, block_size))


def block_mult(field, weights):
    return jnp.einsum("...nc,nce->...ne", field, weights, precision=HIGHEST)


def block_mult_back(field, weights):
    return jnp.einsum("...ne,nce->...nc", field, weights, precision=HIGHEST)


def block_product(real_part, imag_part, weights):
    return (
        block_mult(real_part, weights[0]) - block_mult(imag_part, weights[1]),
        block_mult(real_part, weights[1]) + block_mult(imag_part, weights[0]),
    )


def block_adjoint(real_part, imag_part, weights):
    return (
        block_mult_back(real_part, weights[0]) + block_mult_back(imag_part, weights[1]),
        block_mult_back(imag_part, weights[0]) - block_mult_back(real_part, weights[1]),
    )


def latitude_tables(length):
    index_row = jnp.arange(length, dtype=jnp.int32)
    phase_angle = (
        2.0
        * math.pi
        / length
        * (index_row[:, None] * index_row[None, :] % length).astype(jnp.float32)
    )
    scaling = 1.0 / math.sqrt(length)
    return (jnp.cos(phase_angle) * scaling, -jnp.sin(phase_angle) * scaling)


def to_columns(real_part, imag_part, link_type):
    stacked = jnp.stack([real_part, imag_part]).astype(link_type)
    moved = lax.all_to_all(stacked, "space", 3, 2, tiled=True).astype(jnp.float32)
    return (moved[0], moved[1])


def to_rows(real_part, imag_part, link_type):
    stacked = jnp.stack([real_part, imag_part]).astype(link_type)
    moved = lax.all_to_all(stacked, "space", 2, 3, tiled=True).astype(jnp.float32)
    return (moved[0], moved[1])


def enter_spectrum(real_part, imag_part, tables_lat, link_type=jnp.float32):
    table_cos, table_sin = tables_lat
    real_part, imag_part = to_columns(real_part, imag_part, link_type)
    return complex_latitude(table_cos, table_sin, real_part, imag_part, False)


def leave_spectrum(real_part, imag_part, tables_lat, link_type=jnp.float32):
    table_cos, table_sin = tables_lat
    real_part, imag_part = complex_latitude(table_cos, table_sin, real_part, imag_part, True)
    return to_rows(real_part, imag_part, link_type)


def complex_operator(real_block, imag_block):
    return jnp.stack([jnp.stack([real_block, -imag_block]), jnp.stack([imag_block, real_block])])


def lat_stacked(operator, field, precision=lax.Precision.HIGH):
    return jnp.einsum("pqkh,qbhlc->pbklc", operator, field, precision=precision)


def lon_stacked_forward(field, tables, precision=lax.Precision.HIGH):
    return jnp.einsum("brwc,pwk->pbrkc", field, tables, precision=precision)


def lon_stacked_back(spec, tables, precision=lax.Precision.HIGH):
    return jnp.einsum("pbrkc,pwk->brwc", spec, tables, precision=precision)


def block_operator(weights):
    return jnp.moveaxis(complex_operator(weights[0], weights[1]), 2, 0)


def block_stacked(field, operator):
    return jnp.einsum("qbklnc,npqce->pbklne", field, operator, precision=lax.Precision.HIGH)


def block_stacked_adjoint(field, operator):
    return jnp.einsum("pbklne,npqce->qbklnc", field, operator, precision=lax.Precision.DEFAULT)


def stacked_columns(field, link_type):
    return lax.all_to_all(field.astype(link_type), "space", 3, 2, tiled=True).astype(jnp.float32)


def stacked_rows(field, link_type):
    return lax.all_to_all(field.astype(link_type), "space", 2, 3, tiled=True).astype(jnp.float32)


def token_sums(first_term, second_term):
    pair = jnp.stack([first_term, second_term])
    count = lax.axis_size("feat")
    shifted = jnp.stack(
        [pair]
        + [
            lax.ppermute(pair, "feat", [(i, (i + count - shift) % count) for i in range(count)])
            for shift in range(1, count)
        ]
    )
    total = shifted[0]
    for source in range(1, count):
        total = total + shifted[source]
    return (total[0], total[1])


def ring_send(block):
    count = lax.axis_size("feat")
    return [block] + [
        lax.ppermute(block, "feat", [(i, (i + shift) % count) for i in range(count)])
        for shift in range(1, count)
    ]


def ring_assemble(parts):
    count = len(parts)
    position = lax.axis_index("feat")
    block = parts[0]
    width = block.shape[-1]
    whole = jnp.zeros(block.shape[:-1] + (width * count,), block.dtype)
    for shift, moved in enumerate(parts):
        source = (position + count - shift) % count
        whole = lax.dynamic_update_slice_in_dim(whole, moved, source * width, axis=block.ndim - 1)
    return whole


def channel_share(term):
    return lax.psum_scatter(
        term.astype(jnp.bfloat16), "feat", scatter_dimension=3, tiled=True
    ).astype(jnp.float32)


def gelu_value(field):
    return 0.5 * field * (1.0 + lax.erf(field * (1.0 / math.sqrt(2.0))))


def gelu_slope(field):
    return 0.5 * (1.0 + lax.erf(field * (1.0 / math.sqrt(2.0)))) + field * jnp.exp(
        -0.5 * field * field
    ) * (1.0 / math.sqrt(2.0 * math.pi))


def per_device(inputs, cotangent, spec_w1, spec_b1, spec_w2, spec_b2, up_weight, down_weight):
    full_width = up_weight.shape[0]
    block_size = spec_w1.shape[2]
    tables_lon = padded_tables(inputs.shape[2], lax.axis_size("space"))
    tables_lat = latitude_tables(inputs.shape[1] * lax.axis_size("space"))
    cos_fwd, sin_fwd, cos_inv, sin_inv = tables_lon
    table_cos, table_sin = tables_lat
    operators = (
        jnp.stack([cos_fwd, sin_fwd]),
        jnp.stack([cos_inv, sin_inv]),
        complex_operator(table_cos, table_sin),
        complex_operator(table_cos, -table_sin),
        block_operator(spec_w1),
        block_operator(spec_w2),
    )
    operators = lax.optimization_barrier(operators)
    lon_fwd_tables, lon_inv_tables, lat_forward_op, lat_inverse_op, first_op, second_op = operators
    values = inputs.astype(jnp.float32)
    cotangent_parts = lax.all_gather(cotangent, "feat", axis=3, tiled=True)
    first_sum, second_sum = token_sums(jnp.sum(values, axis=-1), jnp.sum(values * values, axis=-1))
    mean_one = first_sum[..., None] / full_width
    rstd_one = lax.rsqrt(second_sum[..., None] / full_width - mean_one * mean_one + EPSILON)
    normed = (values - mean_one) * rstd_one
    spec = lat_stacked(
        lat_forward_op, stacked_columns(lon_stacked_forward(normed, lon_fwd_tables), jnp.float32)
    )
    spec_blocks = to_blocks(spec, block_size)
    bias_one = to_blocks(spec_b1, block_size)[:, None, None, None]
    bias_two = to_blocks(spec_b2, block_size)[:, None, None, None]
    first = jax.nn.relu(block_stacked(spec_blocks, first_op) + bias_one)
    second = block_stacked(first, second_op) + bias_two
    shrunk = (second - jnp.clip(second, -SHRINK_LEVEL, SHRINK_LEVEL)).reshape(spec.shape)
    shrunk, cotangent_parts = lax.optimization_barrier((shrunk, cotangent_parts))
    whole_cotangent = cotangent_parts
    filtered = lon_stacked_back(
        stacked_rows(lat_stacked(lat_inverse_op, shrunk, lax.Precision.DEFAULT), jnp.bfloat16),
        lon_inv_tables,
        lax.Precision.DEFAULT,
    )
    residual = (filtered + normed + values).astype(jnp.bfloat16)
    residual_vals = residual.astype(jnp.float32)
    whole_residual = lax.all_gather(residual, "feat", axis=3, tiled=True)
    grad_act = jnp.einsum(
        "brwd,hd->brwh", whole_cotangent, down_weight, preferred_element_type=jnp.float32
    )
    whole_residual, grad_act = lax.optimization_barrier((whole_residual, grad_act))
    whole_vals = whole_residual.astype(jnp.float32)
    mean_two = jnp.sum(whole_vals, axis=-1, keepdims=True) / full_width
    square_two = jnp.sum(whole_vals * whole_vals, axis=-1, keepdims=True) / full_width
    rstd_two = lax.rsqrt(square_two - mean_two * mean_two + EPSILON)
    vhat = (whole_vals - mean_two) * rstd_two
    hidden = jnp.einsum(
        "brwd,dh->brwh", vhat.astype(jnp.bfloat16), up_weight, preferred_element_type=jnp.float32
    )
    activated = gelu_value(hidden).astype(jnp.bfloat16)
    mixed_term = jnp.einsum(
        "brwh,hd->brwd", activated, down_weight, preferred_element_type=jnp.float32
    )
    output = (residual_vals + channel_share(mixed_term)).astype(jnp.bfloat16)
    grad_hidden = (grad_act * gelu_slope(hidden)).astype(jnp.bfloat16)
    grad_term = jnp.einsum(
        "brwh,dh->brwd", grad_hidden, up_weight, preferred_element_type=jnp.float32
    )
    total_one, total_two = token_sums(
        jnp.sum(grad_term, axis=-1), jnp.sum(grad_term * vhat, axis=-1)
    )
    grad_vhat = channel_share(grad_term)
    own_hat = (residual_vals - mean_two) * rstd_two
    grad_residual = cotangent.astype(jnp.float32) + rstd_two * (
        grad_vhat
        - total_one[..., None] / full_width
        - own_hat * (total_two[..., None] / full_width)
    )
    grad_spec = lat_stacked(
        lat_forward_op,
        stacked_columns(
            lon_stacked_forward(grad_residual, lon_inv_tables, lax.Precision.DEFAULT), jnp.bfloat16
        ),
        lax.Precision.DEFAULT,
    )
    grad_second = jnp.where(jnp.abs(second) > SHRINK_LEVEL, to_blocks(grad_spec, block_size), 0.0)
    grad_first = jnp.where(first > 0.0, block_stacked_adjoint(grad_second, second_op), 0.0)
    grad_spectrum = block_stacked_adjoint(grad_first, first_op).reshape(spec.shape)
    grad_normed = grad_residual + lon_stacked_back(
        stacked_rows(
            lat_stacked(lat_inverse_op, grad_spectrum, lax.Precision.DEFAULT), jnp.bfloat16
        ),
        lon_fwd_tables,
        lax.Precision.DEFAULT,
    )
    norm_one, norm_two = token_sums(
        jnp.sum(grad_normed, axis=-1), jnp.sum(grad_normed * normed, axis=-1)
    )
    grad_input = grad_residual + rstd_one * (
        grad_normed - norm_one[..., None] / full_width - normed * (norm_two[..., None] / full_width)
    )
    return (output, grad_input.astype(jnp.bfloat16))


def solution(mesh):
    return jax.shard_map(
        per_device,
        mesh=mesh,
        in_specs=(
            P(None, "space", None, "feat"),
            P(None, "space", None, "feat"),
            P(None, "feat", None, None),
            P(None, "feat"),
            P(None, "feat", None, None),
            P(None, "feat"),
            P(None, "feat"),
            P("feat", None),
        ),
        out_specs=(P(None, "space", None, "feat"), P(None, "space", None, "feat")),
        check_vma=False,
    )
```

profile of v0, /device:TPU:1, one launch (start us, length us, event | category | flops | bytes accessed | tf_op | source)
XLA Modules:
  0.0 219.6 jit_solution(13806531281613694137)
XLA Ops:
  7.2 1.7 convert_reduce_fusion.1
  9.0 3.8 %collective-permute-start.1 = (f32[2,2,3,180]{3,2,1,0:T(4,128)S(1)}, f32[2,2,3,180]{3,2,1,0:T(4,128)S(1)}, u32[]{:S(2)}, u32[]{:S(2)}) collective-permute-start(f32[2,2,3,180]{3,2,1,0:T(4,128)S(1)} %pad_maximum_fusion.8), channel_id=1, source_target_pairs={{0,2},{1,3},{2,0},{3,1},{4,6},{5,7},{6,4},{7,5},{8,10},{9,11},{10,... | collective-permute-start | bytes 25928 | tf_op jit(solution)/shard_map/ppermute | solution.py:163
  13.2 2.3 %collective-permute-start = (f32[2,2,3,180]{3,2,1,0:T(4,128)S(1)}, f32[2,2,3,180]{3,2,1,0:T(4,128)S(1)}, u32[]{:S(2)}, u32[]{:S(2)}) collective-permute-start(f32[2,2,3,180]{3,2,1,0:T(4,128)S(1)} %pad_maximum_fusion.8), channel_id=1, source_target_pairs={{0,3},{1,0},{2,1},{3,2},{4,7},{5,4},{6,5},{7,6},{8,11},{9,8},{10,9... | collective-permute-start | bytes 25928 | tf_op jit(solution)/shard_map/ppermute | solution.py:163
  16.8 0.4 fusion.97
  17.4 0.7 pad_maximum_fusion.1
  18.2 1.1 maximum_bitcast_fusion.1
  19.3 0.7 pad_maximum_fusion.3
  20.1 1.0 convolution_bitcast_fusion.7
  21.1 0.9 copy.96
  22.0 28.2 %all_to_all.72 = f32[2,2,3,96,256]{4,1,2,0,3:T(2,128)S(1)} all-to-all(f32[2,2,3,96,256]{4,1,2,0,3:T(2,128)S(1)} %copy.96), channel_id=1, replica_groups=mesh['space'=32,'feat'=4] {'space'}, dimensions={3} | all-to-all | bytes 2359296 | tf_op jit(solution)/shard_map/all_to_all | solution.py:150
  50.6 0.7 convolution_bitcast_fusion.6
  51.3 1.6 reshape.195
  52.9 2.1 fusion.31
  55.1 0.7 fusion.32
  55.7 1.0 copy-done.1
  56.8 1.0 copy_bitcast_fusion
  57.7 1.4 fusion.42
  59.1 0.6 copy.108
  59.8 16.0 %all_to_all.73 = bf16[2,2,96,3,256]{4,0,3,1,2:T(2,128)(2,1)S(1)} all-to-all(bf16[2,2,96,3,256]{4,0,3,1,2:T(2,128)(2,1)S(1)} %copy.108), channel_id=1, replica_groups=mesh['space'=32,'feat'=4] {'space'}, dimensions={2} | all-to-all | bytes 1179648 | tf_op jit(solution)/shard_map/all_to_all | solution.py:154
  75.8 0.5 copy.110
  76.2 1.3 fusion.37
  77.6 6.9 %fusion.16 = f32[2,3,180,1024]{3,2,1,0:T(8,128)} fusion(bf16[2,3,180,1024]{3,0,2,1:T(2,128)(2,1)} %all-gather.3.cloned.1.call-done, bf16[1024,1024]{1,0:T(8,128)(2,1)} %param.15), kind=kOutput, calls=%fused_computation.20 | convolution fusion | flops 2264924160 | bytes 8732672 | tf_op jit(solution)/shard_map/brwd,hd->brwh/dot_general | solution.py:251
  84.5 23.0 %all-gather.5.cloned.1.call-done = bf16[2,3,180,1024]{3,2,1,0:T(8,128)(2,1)} async-done(((bf16[2,3,180,256]{3,2,1,0:T(8,128)(2,1)}), bf16[2,3,180,1024]{3,2,1,0:T(8,128)(2,1)}) %all-gather.5.cloned.1.call-update) | async-done | bytes 2211856 | tf_op jit(solution)/shard_map/all_gather | solution.py:250
  107.6 2.5 %convert_reduce_fusion = (f32[2,3,180]{2,1,0:T(4,128)S(1)}, f32[2,3,180]{2,1,0:T(4,128)S(1)}) fusion(bf16[2,3,180,1024]{3,2,1,0:T(8,128)(2,1)} %all-gather.5.cloned.1.call-done), kind=kLoop, calls=%fused_computation.3 | loop fusion | flops 4421520 | bytes 2220480 | tf_op jit(solution)/shard_map/reduce_sum | solution.py:256
  110.2 2.8 %fusion.14 = f32[2,3,180,1024]{3,2,1,0:T(8,128)S(1)} fusion(bf16[2,3,180,1024]{3,2,1,0:T(8,128)(2,1)S(1)} %copy-done.8, f32[2,3,180]{2,1,0:T(4,128)S(1)} %get-tuple-element.60, f32[2,3,180]{2,1,0:T(4,128)S(1)} %get-tuple-element.59, bf16[1024,1024]{1,0:T(8,128)(2,1)S(1)} %copy-done), kind=kOutput, calls=%fused_computation.19 | convolution fusion | flops 2269347840 | bytes 8741312 | tf_op jit(solution)/shard_map/brwd,dh->brwh/dot_general | solution.py:260
  113.1 5.4 %fusion.123 = (f32[2,3,180]{2,1,0:T(4,128)S(1)}, f32[2,3,180]{2,1,0:T(4,128)S(1)}, bf16[2,3,180,1024]{3,2,1,0:T(8,128)(2,1)}) fusion(f32[2,3,180]{2,1,0:T(4,128)S(1)} %get-tuple-element.60, f32[2,3,180]{2,1,0:T(4,128)S(1)} %get-tuple-element.59, bf16[2,3,180,1024]{3,2,1,0:T(8,128)(2,1)S(1)} %copy-done.8, bf16[1024,1024]{1,0:T(8,128)(2,1)S(1)} %copy-done, ...), kind=kOutput, calls=%fused_computation.189 | convolution fusion | flops 2283722752 | bytes 15385472 | tf_op jit(solution)/shard_map/brwh,dh->brwd/dot_general | solution.py:269
  118.5 6.9 %fusion.28 = bf16[2,3,180,1024]{3,2,1,0:T(8,128)(2,1)} fusion(bf16[1024,1024]{1,0:T(8,128)(2,1)} %param.15, f32[2,3,180,1024]{3,2,1,0:T(8,128)} %copy-done.19), kind=kOutput, calls=%fused_computation.36 | convolution fusion | flops 2271559680 | bytes 8732672 | tf_op jit(solution)/shard_map/brwh,hd->brwd/dot_general | solution.py:264
  125.5 2.5 %collective-permute-start.4 = (f32[2,2,3,180]{3,2,1,0:T(4,128)S(1)}, f32[2,2,3,180]{3,2,1,0:T(4,128)S(1)}, u32[]{:S(2)}, u32[]{:S(2)}) collective-permute-start(f32[2,2,3,180]{3,2,1,0:T(4,128)S(1)} %pad_maximum_fusion.9), channel_id=1, source_target_pairs={{0,2},{1,3},{2,0},{3,1},{4,6},{5,7},{6,4},{7,5},{8,10},{9,11},{10,... | collective-permute-start | bytes 25928 | tf_op jit(solution)/shard_map/ppermute | solution.py:163
  128.0 2.7 %collective-permute-start.3 = (f32[2,2,3,180]{3,2,1,0:T(4,128)S(1)}, f32[2,2,3,180]{3,2,1,0:T(4,128)S(1)}, u32[]{:S(2)}, u32[]{:S(2)}) collective-permute-start(f32[2,2,3,180]{3,2,1,0:T(4,128)S(1)} %pad_maximum_fusion.9), channel_id=1, source_target_pairs={{0,3},{1,0},{2,1},{3,2},{4,7},{5,4},{6,5},{7,6},{8,11},{9,8},{10,9... | collective-permute-start | bytes 25928 | tf_op jit(solution)/shard_map/ppermute | solution.py:163
  130.7 1.3 collective-permute-done.5
  132.0 19.8 %reduce-scatter.5.cloned.1.call-done = bf16[2,3,180,256]{3,2,1,0:T(8,128)(2,1)} async-done(((bf16[2,3,180,1024]{3,2,1,0:T(8,128)(2,1)}), bf16[2,3,180,256]{3,2,1,0:T(8,128)(2,1)}) %reduce-scatter.5.cloned.1.call-update) | async-done | bytes 552976 | tf_op jit(solution)/shard_map/reduce_scatter | solution.py:194
  151.8 2.3 %fusion.40 = bf16[2,2,3,96,256]{4,3,2,1,0:T(8,128)(2,1)S(1)} fusion(bf16[2,180,96]{2,1,0:T(8,128)(2,1)} %pad_maximum_fusion.3, bf16[2,3,180,256]{3,2,1,0:T(8,128)(2,1)} %fusion.37, bf16[2,3,180,256]{3,2,1,0:T(8,128)(2,1)} %reduce-scatter.5.cloned.1.call-done, bf16[2,3,180,256]{3,0,2,1:T(2,128)(2,1)} %param.9, f32[2,3,180]{2,1,0:T(4,128)S(1)} %get-tuple-element.58, ...), kind=kOutput, calls=%fused_computation.61 | convolution fusion | flops 108933120 | bytes 2335104 | tf_op jit(solution)/shard_map/brwc,pwk->pbrkc/dot_general | solution.py:130
  154.1 0.6 copy.114
  154.7 19.7 %all_to_all.74 = bf16[2,2,3,96,256]{4,1,2,0,3:T(2,128)(2,1)S(1)} all-to-all(bf16[2,2,3,96,256]{4,1,2,0,3:T(2,128)(2,1)S(1)} %copy.114), channel_id=1, replica_groups=mesh['space'=32,'feat'=4] {'space'}, dimensions={3} | all-to-all | bytes 1179648 | tf_op jit(solution)/shard_map/all_to_all | solution.py:150
  174.8 1.2 convolution_bitcast_fusion.8
  176.0 2.5 %reshape.229 = bf16[2,2,96,3,2,128]{5,4,2,0,3,1:T(2,128)(2,1)} reshape(bf16[2,2,96,3,256]{4,2,0,3,1:T(8,128)(2,1)} %convolution_bitcast_fusion.8) | data formatting | bytes 1179648 | tf_op jit(solution)/shard_map/reshape | solution.py:60
  178.5 2.1 fusion.39
  181.0 0.6 copy.189
  182.3 0.6 copy.126
  183.0 15.9 %all_to_all.75 = bf16[2,2,96,3,256]{4,0,3,1,2:T(2,128)(2,1)S(1)} all-to-all(bf16[2,2,96,3,256]{4,0,3,1,2:T(2,128)(2,1)S(1)} %copy.126), channel_id=1, replica_groups=mesh['space'=32,'feat'=4] {'space'}, dimensions={2} | all-to-all | bytes 1179648 | tf_op jit(solution)/shard_map/all_to_all | solution.py:154
  198.9 0.5 copy.128
  199.4 2.7 %fusion.124 = (f32[2,3,180]{2,1,0:T(4,128)S(1)}, f32[2,3,180]{2,1,0:T(4,128)S(1)}, f32[2,3,180,256]{3,2,1,0:T(8,128)}) fusion(f32[2,3,180]{2,1,0:T(4,128)S(1)} %fusion.115, f32[2,3,180]{2,1,0:T(4,128)S(1)} %fusion.116, bf16[2,3,180,256]{3,0,2,1:T(2,128)(2,1)S(1)} %copy-done.4, bf16[2,2,3,96,256]{4,1,3,2,0:T(2,128)(2,1)S(1)} %bitcast.284, ...), kind=kOutput, calls=%fused_computation.190 | convolution fusion | flops 110866320 | bytes 4080384 | tf_op jit(solution)/shard_map/pbrkc,pwk->brwc/dot_general | solution.py:134
  202.1 1.3 collective-permute-start.7
  203.4 2.6 %collective-permute-start.6 = (f32[2,2,3,180]{3,2,1,0:T(4,128)S(1)}, f32[2,2,3,180]{3,2,1,0:T(4,128)S(1)}, u32[]{:S(2)}, u32[]{:S(2)}) collective-permute-start(f32[2,2,3,180]{3,2,1,0:T(4,128)S(1)} %pad_maximum_fusion.10), channel_id=1, source_target_pairs={{0,3},{1,0},{2,1},{3,2},{4,7},{5,4},{6,5},{7,6},{8,11},{9,8},{10,9... | collective-permute-start | bytes 25928 | tf_op jit(solution)/shard_map/ppermute | solution.py:163
  206.3 0.9 collective-permute-done.8
  207.3 3.4 %fusion.68 = (bf16[2,3,180,256]{3,2,1,0:T(8,128)(2,1)S(1)}, bf16[2,3,180,256]{3,2,1,0:T(8,128)(2,1)S(1)}) fusion(f32[2,3,180,256]{3,2,1,0:T(8,128)} %get-tuple-element.64, f32[2,3,180]{2,1,0:T(4,128)S(1)} %get-tuple-element.56, f32[2,3,180]{2,1,0:T(4,128)S(1)} %get-tuple-element.55, f32[2,3,180]{2,1,0:T(4,128)S(1)} %fusion.115, ...), kind=kLoop, calls=%fused_computation.92 | loop fusion | flops 6082560 | bytes 5011200 | tf_op jit(solution)/shard_map/convert_element_type | solution.py:305
  210.6 1.2 copy.131
  211.9 1.2 copy.130
  (95 shorter events, 4.5 us)
Async XLA Ops:
  7.2 103.0 %copy-start = (bf16[1024,1024]{1,0:T(8,128)(2,1)S(1)}, bf16[1024,1024]{1,0:T(8,128)(2,1)}, u32[]{:S(2)}) copy-start(bf16[1024,1024]{1,0:T(8,128)(2,1)} %param.14) | copy-start | bytes 6291460
  7.2 10.1 %copy-start.14 = (f32[2,2,128,128]{3,2,1,0:T(8,128)S(1)}, f32[2,2,128,128]{3,2,1,0:T(8,128)}, u32[]{:S(2)}) copy-start(f32[2,2,128,128]{3,2,1,0:T(8,128)} %param.10) | copy-start | bytes 786436
  7.2 50.5 %all-gather.3.cloned.1.call-start = ((), (), s32[]{:S(2)}) async-start(), calls=%async_computation.6 | async-start | bytes 2764800 | tf_op jit(solution)/shard_map/all_gather | solution.py:227
  9.0 8.4 %copy-start.15 = (f32[2,2,128,128]{3,2,1,0:T(8,128)S(1)}, f32[2,2,128,128]{3,2,1,0:T(8,128)}, u32[]{:S(2)}) copy-start(f32[2,2,128,128]{3,2,1,0:T(8,128)} %param.12) | copy-start | bytes 786436
  9.0 11.0 %collective-permute-start.1 = (f32[2,2,3,180]{3,2,1,0:T(4,128)S(1)}, f32[2,2,3,180]{3,2,1,0:T(4,128)S(1)}, u32[]{:S(2)}, u32[]{:S(2)}) collective-permute-start(f32[2,2,3,180]{3,2,1,0:T(4,128)S(1)} %pad_maximum_fusion.8), channel_id=1, source_target_pairs={{0,2},{1,3},{2,0},{3,1},{4,6},{5,7},{6,4},{7,5},{8,10},{9,11},{10,... | collective-permute-start | bytes 25928 | tf_op jit(solution)/shard_map/ppermute | solution.py:163
  12.8 7.2 %collective-permute-start.2 = (f32[2,2,3,180]{3,2,1,0:T(4,128)S(1)}, f32[2,2,3,180]{3,2,1,0:T(4,128)S(1)}, u32[]{:S(2)}, u32[]{:S(2)}) collective-permute-start(f32[2,2,3,180]{3,2,1,0:T(4,128)S(1)} %pad_maximum_fusion.8), channel_id=1, source_target_pairs={{0,1},{1,2},{2,3},{3,0},{4,5},{5,6},{6,7},{7,4},{8,9},{9,10},{10,1... | collective-permute-start | bytes 25928 | tf_op jit(solution)/shard_map/ppermute | solution.py:163
  13.2 6.8 %collective-permute-start = (f32[2,2,3,180]{3,2,1,0:T(4,128)S(1)}, f32[2,2,3,180]{3,2,1,0:T(4,128)S(1)}, u32[]{:S(2)}, u32[]{:S(2)}) collective-permute-start(f32[2,2,3,180]{3,2,1,0:T(4,128)S(1)} %pad_maximum_fusion.8), channel_id=1, source_target_pairs={{0,3},{1,0},{2,1},{3,2},{4,7},{5,4},{6,5},{7,6},{8,11},{9,8},{10,9... | collective-permute-start | bytes 25928 | tf_op jit(solution)/shard_map/ppermute | solution.py:163
  15.5 92.1 %all-gather.5.cloned.1.call-start = ((), (), s32[]{:S(2)}) async-start(), calls=%async_computation.7 | async-start | bytes 2826240 | tf_op jit(solution)/shard_map/all_gather | solution.py:250
  17.4 2.6 %copy-start.11 = (f32[2,180,96]{2,1,0:T(8,128)}, f32[2,180,96]{2,1,0:T(8,128)S(1)}, u32[]{:S(2)}) copy-start(f32[2,180,96]{2,1,0:T(8,128)S(1)} %pad_maximum_fusion.2) | copy-start | bytes 414724
  18.2 1.8 copy-start.2
  51.3 1.6 copy-start.17
  52.9 2.1 copy-start.6
  52.9 2.1 copy-start.18
  55.7 1.0 copy-start.1
  59.8 16.5 %copy-start.3 = (bf16[2,3,180,256]{3,0,2,1:T(2,128)(2,1)S(1)}, bf16[2,3,180,256]{3,0,2,1:T(2,128)(2,1)}, u32[]{:S(2)}) copy-start(bf16[2,3,180,256]{3,0,2,1:T(2,128)(2,1)} %param.8) | copy-start | bytes 1658884
  59.8 16.5 %copy-start.16 = (bf16[2,180,96]{2,1,0:T(8,128)(2,1)S(1)}, bf16[2,180,96]{2,1,0:T(8,128)(2,1)}, u32[]{:S(2)}) copy-start(bf16[2,180,96]{2,1,0:T(8,128)(2,1)} %pad_maximum_fusion.3) | copy-start | bytes 207364
  77.6 74.2 %reduce-scatter.5.cloned.1.call-start = ((), (), s32[]{:S(2)}) async-start(), calls=%async_computation.9 | async-start | bytes 2826240 | tf_op jit(solution)/shard_map/reduce_scatter | solution.py:194
  107.6 2.6 %copy-start.8 = (bf16[2,3,180,1024]{3,2,1,0:T(8,128)(2,1)S(1)}, bf16[2,3,180,1024]{3,2,1,0:T(8,128)(2,1)}, u32[]{:S(2)}) copy-start(bf16[2,3,180,1024]{3,2,1,0:T(8,128)(2,1)} %all-gather.5.cloned.1.call-done) | copy-start | bytes 6635524
  107.6 5.4 %slice-start = ((s8[4521984]{0:T(1024)(128)(4,1)}), s8[4194304]{0:T(1024)(128)(4,1)S(1)}, s32[]{:S(2)}) async-start(s8[4521984]{0:T(1024)(128)(4,1)} %bitcast.300), calls=%async_computation.10 | async-start | bytes 8388608
  110.2 2.9 %slice-start.1 = ((s8[4521984]{0:T(1024)(128)(4,1)}), s8[327680]{0:T(1024)(128)(4,1)S(1)}, s32[]{:S(2)}) async-start(s8[4521984]{0:T(1024)(128)(4,1)} %bitcast.300), calls=%async_computation.11 | async-start | bytes 655360
  113.0 5.4 %copy-start.19 = (f32[2,3,180,1024]{3,2,1,0:T(8,128)}, f32[2,3,180,1024]{3,2,1,0:T(8,128)S(1)}, u32[]{:S(2)}) copy-start(f32[2,3,180,1024]{3,2,1,0:T(8,128)S(1)} %fusion.14) | copy-start | bytes 13271044
  118.5 88.8 %reduce-scatter.3.cloned.1.call-start = ((), (), s32[]{:S(2)}) async-start(), calls=%async_computation.8 | async-start | bytes 2826240 | tf_op jit(solution)/shard_map/reduce_scatter | solution.py:194
  125.5 5.2 %collective-permute-start.4 = (f32[2,2,3,180]{3,2,1,0:T(4,128)S(1)}, f32[2,2,3,180]{3,2,1,0:T(4,128)S(1)}, u32[]{:S(2)}, u32[]{:S(2)}) collective-permute-start(f32[2,2,3,180]{3,2,1,0:T(4,128)S(1)} %pad_maximum_fusion.9), channel_id=1, source_target_pairs={{0,2},{1,3},{2,0},{3,1},{4,6},{5,7},{6,4},{7,5},{8,10},{9,11},{10,... | collective-permute-start | bytes 25928 | tf_op jit(solution)/shard_map/ppermute | solution.py:163
  128.0 4.0 %collective-permute-start.5 = (f32[2,2,3,180]{3,2,1,0:T(4,128)S(1)}, f32[2,2,3,180]{3,2,1,0:T(4,128)S(1)}, u32[]{:S(2)}, u32[]{:S(2)}) collective-permute-start(f32[2,2,3,180]{3,2,1,0:T(4,128)S(1)} %pad_maximum_fusion.9), channel_id=1, source_target_pairs={{0,1},{1,2},{2,3},{3,0},{4,5},{5,6},{6,7},{7,4},{8,9},{9,10},{10,1... | collective-permute-start | bytes 25928 | tf_op jit(solution)/shard_map/ppermute | solution.py:163
  128.0 4.0 %collective-permute-start.3 = (f32[2,2,3,180]{3,2,1,0:T(4,128)S(1)}, f32[2,2,3,180]{3,2,1,0:T(4,128)S(1)}, u32[]{:S(2)}, u32[]{:S(2)}) collective-permute-start(f32[2,2,3,180]{3,2,1,0:T(4,128)S(1)} %pad_maximum_fusion.9), channel_id=1, source_target_pairs={{0,3},{1,0},{2,1},{3,2},{4,7},{5,4},{6,5},{7,6},{8,11},{9,8},{10,9... | collective-permute-start | bytes 25928 | tf_op jit(solution)/shard_map/ppermute | solution.py:163
  178.5 2.1 copy-start.5
  180.9 1.0 copy-start.10
  182.3 17.0 %copy-start.13 = (bf16[2,3,180,256]{3,2,1,0:T(8,128)(2,1)S(1)}, bf16[2,3,180,256]{3,2,1,0:T(8,128)(2,1)}, u32[]{:S(2)}) copy-start(bf16[2,3,180,256]{3,2,1,0:T(8,128)(2,1)} %reduce-scatter.5.cloned.1.call-done) | copy-start | bytes 1658884
  183.0 16.4 %copy-start.4 = (bf16[2,3,180,256]{3,0,2,1:T(2,128)(2,1)S(1)}, bf16[2,3,180,256]{3,0,2,1:T(2,128)(2,1)}, u32[]{:S(2)}) copy-start(bf16[2,3,180,256]{3,0,2,1:T(2,128)(2,1)} %param.8) | copy-start | bytes 1658884
  183.0 16.4 %copy-start.7 = (bf16[2,3,180,256]{3,2,1,0:T(8,128)(2,1)S(1)}, bf16[2,3,180,256]{3,2,1,0:T(8,128)(2,1)}, u32[]{:S(2)}) copy-start(bf16[2,3,180,256]{3,2,1,0:T(8,128)(2,1)} %fusion.37) | copy-start | bytes 1658884
  183.0 16.4 %copy-start.9 = (bf16[2,3,180,256]{3,0,2,1:T(2,128)(2,1)S(1)}, bf16[2,3,180,256]{3,0,2,1:T(2,128)(2,1)}, u32[]{:S(2)}) copy-start(bf16[2,3,180,256]{3,0,2,1:T(2,128)(2,1)} %param.9) | copy-start | bytes 1658884
  183.0 16.4 %copy-start.12 = (f32[2,180,96]{2,1,0:T(8,128)S(1)}, f32[2,180,96]{2,1,0:T(8,128)}, u32[]{:S(2)}) copy-start(f32[2,180,96]{2,1,0:T(8,128)} %copy-done.11) | copy-start | bytes 414724
  202.1 4.2 %collective-permute-start.7 = (f32[2,2,3,180]{3,2,1,0:T(4,128)S(1)}, f32[2,2,3,180]{3,2,1,0:T(4,128)S(1)}, u32[]{:S(2)}, u32[]{:S(2)}) collective-permute-start(f32[2,2,3,180]{3,2,1,0:T(4,128)S(1)} %pad_maximum_fusion.10), channel_id=1, source_target_pairs={{0,2},{1,3},{2,0},{3,1},{4,6},{5,7},{6,4},{7,5},{8,10},{9,11},{10,... | collective-permute-start | bytes 25928 | tf_op jit(solution)/shard_map/ppermute | solution.py:163
  203.4 3.8 %collective-permute-start.8 = (f32[2,2,3,180]{3,2,1,0:T(4,128)S(1)}, f32[2,2,3,180]{3,2,1,0:T(4,128)S(1)}, u32[]{:S(2)}, u32[]{:S(2)}) collective-permute-start(f32[2,2,3,180]{3,2,1,0:T(4,128)S(1)} %pad_maximum_fusion.10), channel_id=1, source_target_pairs={{0,1},{1,2},{2,3},{3,0},{4,5},{5,6},{6,7},{7,4},{8,9},{9,10},{10,1... | collective-permute-start | bytes 25928 | tf_op jit(solution)/shard_map/ppermute | solution.py:163
  203.4 3.8 %collective-permute-start.6 = (f32[2,2,3,180]{3,2,1,0:T(4,128)S(1)}, f32[2,2,3,180]{3,2,1,0:T(4,128)S(1)}, u32[]{:S(2)}, u32[]{:S(2)}) collective-permute-start(f32[2,2,3,180]{3,2,1,0:T(4,128)S(1)} %pad_maximum_fusion.10), channel_id=1, source_target_pairs={{0,3},{1,0},{2,1},{3,2},{4,7},{5,4},{6,5},{7,6},{8,11},{9,8},{10,9... | collective-permute-start | bytes 25928 | tf_op jit(solution)/shard_map/ppermute | solution.py:163
Sparse Core Ops, SparseCore 0:
  15.6 35.1 all-gather.2
  77.7 29.8 all-gather.4
  118.6 33.1 reduce-scatter.4
  154.2 30.7 reduce-scatter.2
where the time goes:
time: 220 us
  blocking collectives  79.8 us (36%)
  waiting for transfers between devices  45.3 us (21%)
  matrix products  38.3 us (17%)
  starting transfers between devices  15.8 us (7%)
  between operations  14.4 us (7%)
  local copies, waits for them, and re-layouts  13.1 us (6%)
  other arithmetic  12.9 us (6%)
    all_to_all x2, blocking collectives, stacked_columns(): lax.all_to_all(field.astype(link_type), 'space', 3, 2, tiled=True)  47.9 us
    all_to_all x2, blocking collectives, stacked_rows(): lax.all_to_all(field.astype(link_type), 'space', 2, 3, tiled=True)  31.9 us
    all_gather x1, waiting for transfers between devices, per_device(): whole_residual = lax.all_gather(residual, 'feat', axis=3, tiled=True)  23 us
    reduce_scatter x2, waiting for transfers between devices, channel_share(): lax.psum_scatter(term.astype(jnp.bfloat16), 'feat', scatter_dimension=3,...  19.8 us
    ppermute x9, starting transfers between devices, token_sums(): lax.ppermute(pair, 'feat', [(i, (i + count - shift) % count) for i in ran...  15.6 us
    dot_general x1, matrix products, per_device(): jnp.einsum('brwd,hd->brwh', whole_cotangent, down_weight, preferred_eleme...  6.92 us
    dot_general x1, matrix products, per_device(): jnp.einsum('brwh,hd->brwd', activated, down_weight, preferred_element_typ...  6.91 us
    dot_general x1, matrix products, per_device(): jnp.einsum('brwh,dh->brwd', grad_hidden, up_weight, preferred_element_typ...  5.41 us
  transfers between devices with their start and end apart: 13, of which 5 were waited for; matrix products, arithmetic and copies ran while one was open for 19% of the time, Pallas kernels for 0%

commit v1 on v0

--- a/solution.py
+++ b/solution.py
@@ -247,7 +247,18 @@
     )
     residual = (filtered + normed + values).astype(jnp.bfloat16)
     residual_vals = residual.astype(jnp.float32)
-    whole_residual = lax.all_gather(residual, "feat", axis=3, tiled=True)
+    ways = lax.axis_size("feat")
+    up = [(d, (d + 1) % ways) for d in range(ways)]
+    down = [(d, (d - 1) % ways) for d in range(ways)]
+    earlier, later = ([residual], [residual])
+    for _ in range(ways // 2):
+        earlier.append(lax.ppermute(earlier[-1], "feat", up))
+    for _ in range((ways - 1) // 2):
+        later.append(lax.ppermute(later[-1], "feat", down))
+    line = jnp.concatenate([*earlier[::-1], *later[1:]], axis=3)
+    whole_residual = jnp.roll(
+        line, (lax.axis_index("feat") - ways // 2) * residual.shape[3], axis=3
+    )
     grad_act = jnp.einsum(
         "brwd,hd->brwh", whole_cotangent, down_weight, preferred_element_type=jnp.float32
     )

time: 220 us -> 223 us (1.014)
  local copies, waits for them, and re-layouts: 13.1 us -> 18.3 us
  matrix products: 38.3 us -> 35.4 us
  starting transfers between devices: 15.8 us -> 18.2 us
    ppermute x0 -> x3, waiting for transfers between devices: none -> 25.8 us  [the longest x2 23.1 us: per_device(): earlier.append(lax.ppermute(earlier[-1], 'feat', up))]
    all_gather x1 -> x0, waiting for transfers between devices: 23 us -> none  [per_device(): whole_residual = lax.all_gather(residual, 'feat', axis=3, tiled=True)]
    unnamed x46 -> x51, local copies, waits for them, and re-layouts: 3.58 us -> 7.09 us
    reduce_scatter x2, waiting for transfers between devices: 19.8 us -> 16.9 us  [channel_share(): lax.psum_scatter(term.astype(jnp.bfloat16), 'feat', scatter_dimension=3,...]
    ppermute x0 -> x3, starting transfers between devices: none -> 2.75 us  [the longest x1 2.74 us: per_device(): later.append(lax.ppermute(later[-1], 'feat', down))]
  transfers between devices with their start and end apart: 13 -> 15, of which waited for: 5 -> 8; matrix products, arithmetic and copies ran while one was open for 19% -> 18% of each run, Pallas kernels for 0% -> 0%
where the time goes in v1:
time: 223 us
  blocking collectives  79.1 us (35%)
  waiting for transfers between devices  46.3 us (21%)
  matrix products  35.4 us (16%)
  local copies, waits for them, and re-layouts  18.3 us (8%)
  starting transfers between devices  18.2 us (8%)
  between operations  14.4 us (6%)
  other arithmetic  11.1 us (5%)
    all_to_all x2, blocking collectives, stacked_columns(): lax.all_to_all(field.astype(link_type), 'space', 3, 2, tiled=True)  47.2 us
    all_to_all x2, blocking collectives, stacked_rows(): lax.all_to_all(field.astype(link_type), 'space', 2, 3, tiled=True)  31.9 us
    ppermute x2, waiting for transfers between devices, per_device(): earlier.append(lax.ppermute(earlier[-1], 'feat', up))  23.1 us
    reduce_scatter x2, waiting for transfers between devices, channel_share(): lax.psum_scatter(term.astype(jnp.bfloat16), 'feat', scatter_dimension=3,...  16.9 us
    ppermute x9, starting transfers between devices, token_sums(): lax.ppermute(pair, 'feat', [(i, (i + count - shift) % count) for i in ran...  15.4 us
    unnamed x51, local copies, waits for them, and re-layouts  7.09 us
    dot_general x1, matrix products, per_device(): jnp.einsum('brwh,hd->brwd', activated, down_weight, preferred_element_typ...  6.9 us
    dot_general x1, matrix products, per_device(): jnp.einsum('brwh,dh->brwd', grad_hidden, up_weight, preferred_element_typ...  5.39 us
  transfers between devices with their start and end apart: 15, of which 8 were waited for; matrix products, arithmetic and copies ran while one was open for 18% of the time, Pallas kernels for 0%

profile of v1, /device:TPU:1, one launch (start us, length us, event | category | flops | bytes accessed | tf_op | source)
XLA Modules:
  0.0 222.8 jit_solution(9171462494656538538)
XLA Ops:
  7.2 1.7 convert_reduce_fusion.1
  9.0 3.8 %collective-permute-start.1 = (f32[2,2,3,180]{3,2,1,0:T(4,128)S(1)}, f32[2,2,3,180]{3,2,1,0:T(4,128)S(1)}, u32[]{:S(2)}, u32[]{:S(2)}) collective-permute-start(f32[2,2,3,180]{3,2,1,0:T(4,128)S(1)} %pad_maximum_fusion.8), channel_id=1, source_target_pairs={{0,2},{1,3},{2,0},{3,1},{4,6},{5,7},{6,4},{7,5},{8,10},{9,11},{10,... | collective-permute-start | bytes 25928 | tf_op jit(solution)/shard_map/ppermute | solution.py:163
  13.2 2.3 %collective-permute-start = (f32[2,2,3,180]{3,2,1,0:T(4,128)S(1)}, f32[2,2,3,180]{3,2,1,0:T(4,128)S(1)}, u32[]{:S(2)}, u32[]{:S(2)}) collective-permute-start(f32[2,2,3,180]{3,2,1,0:T(4,128)S(1)} %pad_maximum_fusion.8), channel_id=1, source_target_pairs={{0,3},{1,0},{2,1},{3,2},{4,7},{5,4},{6,5},{7,6},{8,11},{9,8},{10,9... | collective-permute-start | bytes 25928 | tf_op jit(solution)/shard_map/ppermute | solution.py:163
  17.4 0.7 pad_maximum_fusion.1
  18.3 1.1 maximum_bitcast_fusion.1
  20.1 1.0 convolution_bitcast_fusion.7
  21.1 0.9 copy.104
  22.0 28.2 %all_to_all.72 = f32[2,2,3,96,256]{4,1,2,0,3:T(2,128)S(1)} all-to-all(f32[2,2,3,96,256]{4,1,2,0,3:T(2,128)S(1)} %copy.104), channel_id=1, replica_groups=mesh['space'=32,'feat'=4] {'space'}, dimensions={3} | all-to-all | bytes 2359296 | tf_op jit(solution)/shard_map/all_to_all | solution.py:150
  50.6 0.7 convolution_bitcast_fusion.6
  51.3 1.6 reshape.195
  52.9 2.1 fusion.31
  55.1 0.6 fusion.32
  55.7 1.0 copy-done.1
  56.7 1.0 copy_bitcast_fusion
  57.7 1.4 fusion.42
  59.8 16.0 %all_to_all.73 = bf16[2,2,96,3,256]{4,0,3,1,2:T(2,128)(2,1)S(1)} all-to-all(bf16[2,2,96,3,256]{4,0,3,1,2:T(2,128)(2,1)S(1)} %copy.116), channel_id=1, replica_groups=mesh['space'=32,'feat'=4] {'space'}, dimensions={2} | all-to-all | bytes 1179648 | tf_op jit(solution)/shard_map/all_to_all | solution.py:154
  76.7 0.8 copy-done.2
  77.5 1.2 copy.120
  78.8 15.9 %collective-permute-done.3 = bf16[2,3,180,256]{3,0,2,1:T(2,128)(2,1)} collective-permute-done((bf16[2,3,180,256]{3,0,2,1:T(2,128)(2,1)}, bf16[2,3,180,256]{3,0,2,1:T(2,128)(2,1)}, u32[]{:S(2)}, u32[]{:S(2)}) %collective-permute-start.3) | collective-permute-done | bytes 552992 | tf_op jit(solution)/shard_map/ppermute | solution.py:255
  94.6 4.8 %fusion.16 = f32[2,3,180,1024]{3,2,1,0:T(8,128)S(1)} fusion(bf16[2,3,180,1024]{3,0,2,1:T(2,128)(2,1)} %all-gather.2.cloned.1.call-done, bf16[1024,1024]{1,0:T(8,128)(2,1)} %param.15), kind=kOutput, calls=%fused_computation.20 | convolution fusion | flops 2264924160 | bytes 8732672 | tf_op jit(solution)/shard_map/brwd,hd->brwh/dot_general | solution.py:262
  99.5 2.7 %collective-permute-start.5 = (bf16[2,3,180,256]{3,0,2,1:T(2,128)(2,1)}, bf16[2,3,180,256]{3,0,2,1:T(2,128)(2,1)S(1)}, u32[]{:S(2)}, u32[]{:S(2)}) collective-permute-start(bf16[2,3,180,256]{3,0,2,1:T(2,128)(2,1)} %copy.120), channel_id=1, source_target_pairs={{0,3},{1,0},{2,1},{3,2},{4,7},{5,4},{6,5},{7,6},{8,11},{9,8},{10,9... | collective-permute-start | bytes 1658888 | tf_op jit(solution)/shard_map/ppermute | solution.py:257
  102.2 7.3 %collective-permute-done.4 = bf16[2,3,180,256]{3,0,2,1:T(2,128)(2,1)S(1)} collective-permute-done((bf16[2,3,180,256]{3,0,2,1:T(2,128)(2,1)}, bf16[2,3,180,256]{3,0,2,1:T(2,128)(2,1)S(1)}, u32[]{:S(2)}, u32[]{:S(2)}) %collective-permute-start.4) | collective-permute-done | bytes 552992 | tf_op jit(solution)/shard_map/ppermute | solution.py:255
  109.6 1.2 copy_dynamic-update-slice_fusion.2
  110.8 2.6 %collective-permute-done.5 = bf16[2,3,180,256]{3,0,2,1:T(2,128)(2,1)S(1)} collective-permute-done((bf16[2,3,180,256]{3,0,2,1:T(2,128)(2,1)}, bf16[2,3,180,256]{3,0,2,1:T(2,128)(2,1)S(1)}, u32[]{:S(2)}, u32[]{:S(2)}) %collective-permute-start.5) | collective-permute-done | bytes 552992 | tf_op jit(solution)/shard_map/ppermute | solution.py:257
  113.7 1.2 copy_dynamic-update-slice_fusion.3
  115.3 0.7 convert_reduce_fusion
  116.1 2.8 %fusion.14 = f32[2,3,180,1024]{3,2,1,0:T(8,128)S(1)} fusion(bf16[2,3,180,1024]{3,2,1,0:T(8,128)(2,1)S(1)} %constant_dynamic-slice_fusion, f32[2,3,180]{2,1,0:T(4,128)S(1)} %get-tuple-element.60, f32[2,3,180]{2,1,0:T(4,128)S(1)} %get-tuple-element.59, bf16[1024,1024]{1,0:T(8,128)(2,1)S(1)} %copy-done), kind=kOutput, calls=%fused_computation.19 | convolution fusion | flops 2269347840 | bytes 8741312 | tf_op jit(solution)/shard_map/brwd,dh->brwh/dot_general | solution.py:271
  118.9 5.4 %fusion.123 = (f32[2,3,180]{2,1,0:T(4,128)S(1)}, f32[2,3,180]{2,1,0:T(4,128)S(1)}, bf16[2,3,180,1024]{3,2,1,0:T(8,128)(2,1)}) fusion(f32[2,3,180]{2,1,0:T(4,128)S(1)} %get-tuple-element.60, f32[2,3,180]{2,1,0:T(4,128)S(1)} %get-tuple-element.59, bf16[2,3,180,1024]{3,2,1,0:T(8,128)(2,1)S(1)} %constant_dynamic-slice_fusion, ...), kind=kOutput, calls=%fused_computation.198 | convolution fusion | flops 2283722752 | bytes 15385472 | tf_op jit(solution)/shard_map/brwh,dh->brwd/dot_general | solution.py:280
  124.4 6.9 %fusion.28 = bf16[2,3,180,1024]{3,2,1,0:T(8,128)(2,1)} fusion(bf16[1024,1024]{1,0:T(8,128)(2,1)} %param.15, f32[2,3,180,1024]{3,2,1,0:T(8,128)} %copy-done.20), kind=kOutput, calls=%fused_computation.36 | convolution fusion | flops 2271559680 | bytes 8732672 | tf_op jit(solution)/shard_map/brwh,hd->brwd/dot_general | solution.py:275
  131.4 2.1 collective-permute-start.7
  133.5 1.8 collective-permute-start.8
  135.3 0.9 collective-permute-start.6
  136.2 1.7 collective-permute-done.8
  137.9 0.7 collective-permute-done.6
  138.6 16.9 %reduce-scatter.5.cloned.1.call-done = bf16[2,3,180,256]{3,2,1,0:T(8,128)(2,1)} async-done(((bf16[2,3,180,1024]{3,2,1,0:T(8,128)(2,1)}), bf16[2,3,180,256]{3,2,1,0:T(8,128)(2,1)}) %reduce-scatter.5.cloned.1.call-update) | async-done | bytes 552976 | tf_op jit(solution)/shard_map/reduce_scatter | solution.py:194
  155.5 2.3 %fusion.40 = bf16[2,2,3,96,256]{4,3,2,1,0:T(8,128)(2,1)S(1)} fusion(bf16[2,180,96]{2,1,0:T(8,128)(2,1)} %pad_maximum_fusion.3, bf16[2,3,180,256]{3,2,1,0:T(8,128)(2,1)} %copy-done.2, bf16[2,3,180,256]{3,2,1,0:T(8,128)(2,1)} %reduce-scatter.5.cloned.1.call-done, bf16[2,3,180,256]{3,0,2,1:T(2,128)(2,1)} %param.9, f32[2,3,180]{2,1,0:T(4,128)S(1)} %get-tuple-element.58, ...), kind=kOutput, calls=%fused_computation.61 | convolution fusion | flops 108933120 | bytes 2335104 | tf_op jit(solution)/shard_map/brwc,pwk->pbrkc/dot_general | solution.py:130
  158.5 19.0 %all_to_all.74 = bf16[2,2,3,96,256]{4,1,2,0,3:T(2,128)(2,1)S(1)} all-to-all(bf16[2,2,3,96,256]{4,1,2,0,3:T(2,128)(2,1)S(1)} %copy.130), channel_id=1, replica_groups=mesh['space'=32,'feat'=4] {'space'}, dimensions={3} | all-to-all | bytes 1179648 | tf_op jit(solution)/shard_map/all_to_all | solution.py:150
  177.9 1.2 convolution_bitcast_fusion.8
  179.1 2.5 %reshape.229 = bf16[2,2,96,3,2,128]{5,4,2,0,3,1:T(2,128)(2,1)} reshape(bf16[2,2,96,3,256]{4,2,0,3,1:T(8,128)(2,1)} %convolution_bitcast_fusion.8) | data formatting | bytes 1179648 | tf_op jit(solution)/shard_map/reshape | solution.py:60
  181.6 2.1 fusion.39
  186.1 15.9 %all_to_all.75 = bf16[2,2,96,3,256]{4,0,3,1,2:T(2,128)(2,1)S(1)} all-to-all(bf16[2,2,96,3,256]{4,0,3,1,2:T(2,128)(2,1)S(1)} %copy.142), channel_id=1, replica_groups=mesh['space'=32,'feat'=4] {'space'}, dimensions={2} | all-to-all | bytes 1179648 | tf_op jit(solution)/shard_map/all_to_all | solution.py:154
  202.5 2.8 %fusion.124 = (f32[2,3,180]{2,1,0:T(4,128)S(1)}, f32[2,3,180]{2,1,0:T(4,128)S(1)}, f32[2,3,180,256]{3,2,1,0:T(8,128)}) fusion(f32[2,3,180]{2,1,0:T(4,128)S(1)} %fusion.115, f32[2,3,180]{2,1,0:T(4,128)S(1)} %fusion.116, bf16[2,3,180,256]{3,0,2,1:T(2,128)(2,1)S(1)} %copy-done.7, bf16[2,2,3,96,256]{4,1,3,2,0:T(2,128)(2,1)S(1)} %bitcast.284, ...), kind=kOutput, calls=%fused_computation.199 | convolution fusion | flops 110866320 | bytes 4080384 | tf_op jit(solution)/shard_map/pbrkc,pwk->brwc/dot_general | solution.py:134
  205.2 1.4 collective-permute-start.10
  206.6 2.7 %collective-permute-start.9 = (f32[2,2,3,180]{3,2,1,0:T(4,128)S(1)}, f32[2,2,3,180]{3,2,1,0:T(4,128)S(1)}, u32[]{:S(2)}, u32[]{:S(2)}) collective-permute-start(f32[2,2,3,180]{3,2,1,0:T(4,128)S(1)} %pad_maximum_fusion.10), channel_id=1, source_target_pairs={{0,3},{1,0},{2,1},{3,2},{4,7},{5,4},{6,5},{7,6},{8,11},{9,8},{10,9... | collective-permute-start | bytes 25928 | tf_op jit(solution)/shard_map/ppermute | solution.py:163
  209.4 1.0 collective-permute-done.11
  210.5 3.4 %fusion.68 = (bf16[2,3,180,256]{3,2,1,0:T(8,128)(2,1)S(1)}, bf16[2,3,180,256]{3,2,1,0:T(8,128)(2,1)S(1)}) fusion(f32[2,3,180,256]{3,2,1,0:T(8,128)} %get-tuple-element.64, f32[2,3,180]{2,1,0:T(4,128)S(1)} %get-tuple-element.56, f32[2,3,180]{2,1,0:T(4,128)S(1)} %get-tuple-element.55, f32[2,3,180]{2,1,0:T(4,128)S(1)} %fusion.115, ...), kind=kLoop, calls=%fused_computation.92 | loop fusion | flops 6082560 | bytes 5011200 | tf_op jit(solution)/shard_map/convert_element_type | solution.py:316
  213.8 1.2 copy.147
  215.1 1.2 copy.146
  (105 shorter events, 10.0 us)
Async XLA Ops:
  7.2 108.9 %copy-start = (bf16[1024,1024]{1,0:T(8,128)(2,1)S(1)}, bf16[1024,1024]{1,0:T(8,128)(2,1)}, u32[]{:S(2)}) copy-start(bf16[1024,1024]{1,0:T(8,128)(2,1)} %param.14) | copy-start | bytes 6291460
  7.2 10.1 %copy-start.15 = (f32[2,2,128,128]{3,2,1,0:T(8,128)S(1)}, f32[2,2,128,128]{3,2,1,0:T(8,128)}, u32[]{:S(2)}) copy-start(f32[2,2,128,128]{3,2,1,0:T(8,128)} %param.10) | copy-start | bytes 786436
  7.2 50.5 %all-gather.2.cloned.1.call-start = ((), (), s32[]{:S(2)}) async-start(), calls=%async_computation.6 | async-start | bytes 2764800 | tf_op jit(solution)/shard_map/all_gather | solution.py:227
  9.0 8.4 %copy-start.16 = (f32[2,2,128,128]{3,2,1,0:T(8,128)S(1)}, f32[2,2,128,128]{3,2,1,0:T(8,128)}, u32[]{:S(2)}) copy-start(f32[2,2,128,128]{3,2,1,0:T(8,128)} %param.12) | copy-start | bytes 786436
  9.0 11.0 %collective-permute-start.1 = (f32[2,2,3,180]{3,2,1,0:T(4,128)S(1)}, f32[2,2,3,180]{3,2,1,0:T(4,128)S(1)}, u32[]{:S(2)}, u32[]{:S(2)}) collective-permute-start(f32[2,2,3,180]{3,2,1,0:T(4,128)S(1)} %pad_maximum_fusion.8), channel_id=1, source_target_pairs={{0,2},{1,3},{2,0},{3,1},{4,6},{5,7},{6,4},{7,5},{8,10},{9,11},{10,... | collective-permute-start | bytes 25928 | tf_op jit(solution)/shard_map/ppermute | solution.py:163
  12.8 7.2 %collective-permute-start.2 = (f32[2,2,3,180]{3,2,1,0:T(4,128)S(1)}, f32[2,2,3,180]{3,2,1,0:T(4,128)S(1)}, u32[]{:S(2)}, u32[]{:S(2)}) collective-permute-start(f32[2,2,3,180]{3,2,1,0:T(4,128)S(1)} %pad_maximum_fusion.8), channel_id=1, source_target_pairs={{0,1},{1,2},{2,3},{3,0},{4,5},{5,6},{6,7},{7,4},{8,9},{9,10},{10,1... | collective-permute-start | bytes 25928 | tf_op jit(solution)/shard_map/ppermute | solution.py:163
  13.2 6.8 %collective-permute-start = (f32[2,2,3,180]{3,2,1,0:T(4,128)S(1)}, f32[2,2,3,180]{3,2,1,0:T(4,128)S(1)}, u32[]{:S(2)}, u32[]{:S(2)}) collective-permute-start(f32[2,2,3,180]{3,2,1,0:T(4,128)S(1)} %pad_maximum_fusion.8), channel_id=1, source_target_pairs={{0,3},{1,0},{2,1},{3,2},{4,7},{5,4},{6,5},{7,6},{8,11},{9,8},{10,9... | collective-permute-start | bytes 25928 | tf_op jit(solution)/shard_map/ppermute | solution.py:163
  15.5 140.0 %reduce-scatter.5.cloned.1.call-start = ((), (), s32[]{:S(2)}) async-start(), calls=%async_computation.8 | async-start | bytes 2826240 | tf_op jit(solution)/shard_map/reduce_scatter | solution.py:194
  17.4 2.6 %copy-start.12 = (f32[2,180,96]{2,1,0:T(8,128)}, f32[2,180,96]{2,1,0:T(8,128)S(1)}, u32[]{:S(2)}) copy-start(f32[2,180,96]{2,1,0:T(8,128)S(1)} %pad_maximum_fusion.2) | copy-start | bytes 414724
  18.2 1.8 copy-start.5
  51.3 1.6 copy-start.18
  52.9 2.1 copy-start.9
  52.9 2.1 copy-start.19
  55.7 1.0 copy-start.1
  59.7 16.5 %copy-start.6 = (bf16[2,3,180,256]{3,0,2,1:T(2,128)(2,1)S(1)}, bf16[2,3,180,256]{3,0,2,1:T(2,128)(2,1)}, u32[]{:S(2)}) copy-start(bf16[2,3,180,256]{3,0,2,1:T(2,128)(2,1)} %param.8) | copy-start | bytes 1658884
  59.7 16.5 %copy-start.17 = (bf16[2,180,96]{2,1,0:T(8,128)(2,1)S(1)}, bf16[2,180,96]{2,1,0:T(8,128)(2,1)}, u32[]{:S(2)}) copy-start(bf16[2,180,96]{2,1,0:T(8,128)(2,1)} %pad_maximum_fusion.3) | copy-start | bytes 207364
  76.7 0.8 copy-start.2
  78.8 15.9 %collective-permute-start.3 = (bf16[2,3,180,256]{3,0,2,1:T(2,128)(2,1)}, bf16[2,3,180,256]{3,0,2,1:T(2,128)(2,1)}, u32[]{:S(2)}, u32[]{:S(2)}) collective-permute-start(bf16[2,3,180,256]{3,0,2,1:T(2,128)(2,1)} %copy.120), channel_id=1, source_target_pairs={{0,1},{1,2},{2,3},{3,0},{4,5},{5,6},{6,7},{7,4},{8,9},{9,10},{10,1... | collective-permute-start | bytes 1658888 | tf_op jit(solution)/shard_map/ppermute | solution.py:255
  94.6 14.9 %collective-permute-start.4 = (bf16[2,3,180,256]{3,0,2,1:T(2,128)(2,1)}, bf16[2,3,180,256]{3,0,2,1:T(2,128)(2,1)S(1)}, u32[]{:S(2)}, u32[]{:S(2)}) collective-permute-start(bf16[2,3,180,256]{3,0,2,1:T(2,128)(2,1)} %collective-permute-done.3), channel_id=1, source_target_pairs={{0,1},{1,2},{2,3},{3,0},{4,5},{5,6},{6,7},{7,4},{8,9},{9,10},{10,1... | collective-permute-start | bytes 1658888 | tf_op jit(solution)/shard_map/ppermute | solution.py:255
  99.4 11.3 %copy-start.3 = (bf16[2,3,180,256]{3,2,1,0:T(8,128)(2,1)S(1)}, bf16[2,3,180,256]{3,2,1,0:T(8,128)(2,1)}, u32[]{:S(2)}) copy-start(bf16[2,3,180,256]{3,2,1,0:T(8,128)(2,1)} %copy-done.2) | copy-start | bytes 1658884
  99.5 14.0 %collective-permute-start.5 = (bf16[2,3,180,256]{3,0,2,1:T(2,128)(2,1)}, bf16[2,3,180,256]{3,0,2,1:T(2,128)(2,1)S(1)}, u32[]{:S(2)}, u32[]{:S(2)}) collective-permute-start(bf16[2,3,180,256]{3,0,2,1:T(2,128)(2,1)} %copy.120), channel_id=1, source_target_pairs={{0,3},{1,0},{2,1},{3,2},{4,7},{5,4},{6,5},{7,6},{8,11},{9,8},{10,9... | collective-permute-start | bytes 1658888 | tf_op jit(solution)/shard_map/ppermute | solution.py:257
  118.9 5.4 %copy-start.20 = (f32[2,3,180,1024]{3,2,1,0:T(8,128)}, f32[2,3,180,1024]{3,2,1,0:T(8,128)S(1)}, u32[]{:S(2)}) copy-start(f32[2,3,180,1024]{3,2,1,0:T(8,128)S(1)} %fusion.14) | copy-start | bytes 13271044
  124.4 86.1 %reduce-scatter.3.cloned.1.call-start = ((), (), s32[]{:S(2)}) async-start(), calls=%async_computation.7 | async-start | bytes 2826240 | tf_op jit(solution)/shard_map/reduce_scatter | solution.py:194
  131.4 4.8 %collective-permute-start.7 = (f32[2,2,3,180]{3,2,1,0:T(4,128)S(1)}, f32[2,2,3,180]{3,2,1,0:T(4,128)S(1)}, u32[]{:S(2)}, u32[]{:S(2)}) collective-permute-start(f32[2,2,3,180]{3,2,1,0:T(4,128)S(1)} %pad_maximum_fusion.9), channel_id=1, source_target_pairs={{0,2},{1,3},{2,0},{3,1},{4,6},{5,7},{6,4},{7,5},{8,10},{9,11},{10,... | collective-permute-start | bytes 25928 | tf_op jit(solution)/shard_map/ppermute | solution.py:163
  133.5 4.4 %collective-permute-start.8 = (f32[2,2,3,180]{3,2,1,0:T(4,128)S(1)}, f32[2,2,3,180]{3,2,1,0:T(4,128)S(1)}, u32[]{:S(2)}, u32[]{:S(2)}) collective-permute-start(f32[2,2,3,180]{3,2,1,0:T(4,128)S(1)} %pad_maximum_fusion.9), channel_id=1, source_target_pairs={{0,1},{1,2},{2,3},{3,0},{4,5},{5,6},{6,7},{7,4},{8,9},{9,10},{10,1... | collective-permute-start | bytes 25928 | tf_op jit(solution)/shard_map/ppermute | solution.py:163
  135.3 3.3 %collective-permute-start.6 = (f32[2,2,3,180]{3,2,1,0:T(4,128)S(1)}, f32[2,2,3,180]{3,2,1,0:T(4,128)S(1)}, u32[]{:S(2)}, u32[]{:S(2)}) collective-permute-start(f32[2,2,3,180]{3,2,1,0:T(4,128)S(1)} %pad_maximum_fusion.9), channel_id=1, source_target_pairs={{0,3},{1,0},{2,1},{3,2},{4,7},{5,4},{6,5},{7,6},{8,11},{9,8},{10,9... | collective-permute-start | bytes 25928 | tf_op jit(solution)/shard_map/ppermute | solution.py:163
  181.6 2.1 copy-start.8
  184.0 1.0 copy-start.11
  185.4 17.0 %copy-start.14 = (bf16[2,3,180,256]{3,2,1,0:T(8,128)(2,1)S(1)}, bf16[2,3,180,256]{3,2,1,0:T(8,128)(2,1)}, u32[]{:S(2)}) copy-start(bf16[2,3,180,256]{3,2,1,0:T(8,128)(2,1)} %reduce-scatter.5.cloned.1.call-done) | copy-start | bytes 1658884
  186.0 16.4 %copy-start.4 = (bf16[2,3,180,256]{3,2,1,0:T(8,128)(2,1)S(1)}, bf16[2,3,180,256]{3,2,1,0:T(8,128)(2,1)}, u32[]{:S(2)}) copy-start(bf16[2,3,180,256]{3,2,1,0:T(8,128)(2,1)} %copy-done.2) | copy-start | bytes 1658884
  186.0 16.4 %copy-start.7 = (bf16[2,3,180,256]{3,0,2,1:T(2,128)(2,1)S(1)}, bf16[2,3,180,256]{3,0,2,1:T(2,128)(2,1)}, u32[]{:S(2)}) copy-start(bf16[2,3,180,256]{3,0,2,1:T(2,128)(2,1)} %param.8) | copy-start | bytes 1658884
  186.1 16.4 %copy-start.10 = (bf16[2,3,180,256]{3,0,2,1:T(2,128)(2,1)S(1)}, bf16[2,3,180,256]{3,0,2,1:T(2,128)(2,1)}, u32[]{:S(2)}) copy-start(bf16[2,3,180,256]{3,0,2,1:T(2,128)(2,1)} %param.9) | copy-start | bytes 1658884
  186.1 16.4 %copy-start.13 = (f32[2,180,96]{2,1,0:T(8,128)S(1)}, f32[2,180,96]{2,1,0:T(8,128)}, u32[]{:S(2)}) copy-start(f32[2,180,96]{2,1,0:T(8,128)} %copy-done.12) | copy-start | bytes 414724
  205.2 4.2 %collective-permute-start.10 = (f32[2,2,3,180]{3,2,1,0:T(4,128)S(1)}, f32[2,2,3,180]{3,2,1,0:T(4,128)S(1)}, u32[]{:S(2)}, u32[]{:S(2)}) collective-permute-start(f32[2,2,3,180]{3,2,1,0:T(4,128)S(1)} %pad_maximum_fusion.10), channel_id=1, source_target_pairs={{0,2},{1,3},{2,0},{3,1},{4,6},{5,7},{6,4},{7,5},{8,10},{9,11},{10,... | collective-permute-start | bytes 25928 | tf_op jit(solution)/shard_map/ppermute | solution.py:163
  206.6 3.8 %collective-permute-start.11 = (f32[2,2,3,180]{3,2,1,0:T(4,128)S(1)}, f32[2,2,3,180]{3,2,1,0:T(4,128)S(1)}, u32[]{:S(2)}, u32[]{:S(2)}) collective-permute-start(f32[2,2,3,180]{3,2,1,0:T(4,128)S(1)} %pad_maximum_fusion.10), channel_id=1, source_target_pairs={{0,1},{1,2},{2,3},{3,0},{4,5},{5,6},{6,7},{7,4},{8,9},{9,10},{10,1... | collective-permute-start | bytes 25928 | tf_op jit(solution)/shard_map/ppermute | solution.py:163
  206.6 3.8 %collective-permute-start.9 = (f32[2,2,3,180]{3,2,1,0:T(4,128)S(1)}, f32[2,2,3,180]{3,2,1,0:T(4,128)S(1)}, u32[]{:S(2)}, u32[]{:S(2)}) collective-permute-start(f32[2,2,3,180]{3,2,1,0:T(4,128)S(1)} %pad_maximum_fusion.10), channel_id=1, source_target_pairs={{0,3},{1,0},{2,1},{3,2},{4,7},{5,4},{6,5},{7,6},{8,11},{9,8},{10,9... | collective-permute-start | bytes 25928 | tf_op jit(solution)/shard_map/ppermute | solution.py:163
Sparse Core Ops, SparseCore 0:
  15.6 35.1 all-gather.1
  124.5 30.9 reduce-scatter.4
  158.1 30.1 reduce-scatter.2
